TPU v7x, 128 devices: a whole 4x4x4 slice. The times are simulated.
128 devices in a mesh: cube: 2 (over y_hi), front: 16 (over y_lo, x, core), col: 4 (over z).
Axes of the slice: x: 4, y: 4 (y_hi: 2, y_lo: 2; y = y_hi * 2 + y_lo), z: 4, core: 2. Of those that a mesh axis runs over, the one named last changes fastest.
Arguments:
- parent_front: float32 [8192, 8192], P(('cube', 'front'), 'col'), may hold values from -16 to 18, as said below
- child_blocks: bfloat16 [2, 6144, 6144], P('cube', 'front'), may hold values from -16 to 16, as said below
- row_maps: int32 [2, 6144], replicated, may hold values from 0 to 8191, as said below
- front_size: int32 [1], replicated, may hold values from 6144 to 8192
Outputs:
- factor: float32 [8192, 512], P(('cube', 'front'))
- schur: float32 [8192, 8192], P(('cube', 'front'), 'col')
Inputs may be any that keep to these rules, and one draw needn't show every extreme that they name: `parent_front`: symmetric, and the assembled front is positive definite. `child_blocks`: each child's block is symmetric. For each child c and index i, with g = i // 192, row_maps[c, i] lies in the front rows b * 256 to (b + 1) * 256 - 1, where b = (g % 2) * 16 + g // 2; one child's entries are distinct and rise within each run of 192.
All inputs are finite; a program needn't handle non-finite values.
Results may differ from a plain program's by a relative error of at most 0.0003.
Values may be sent and summed in bfloat16 or wider, within the bound.
No kernel may reach another device: no remote copies, remote signals or barrier semaphores. Data moves between devices by JAX's collectives and lax.ppermute only.
A program may use at most 64 MiB of HBM per device.

v0:
```python
import jax
import jax.numpy as jnp
from jax import lax
from jax.sharding import PartitionSpec as P

PW = 256
NP = 2
K = 512


def swapped(shard, axis, distance):
    return lax.ppermute(shard, axis, [(i, i ^ 1 << distance) for i in range(lax.axis_size(axis))])


def spread(block, axis, owner):
    block = jnp.where(lax.axis_index(axis) == owner, block, jnp.zeros_like(block))
    return lax.psum(block, axis)


def place_columns(part, column_map, col_start, width):
    local = column_map - col_start
    inside = (local >= 0) & (local < width)
    target = jnp.where(inside, local, width)
    placed = jnp.zeros((part.shape[0], width), part.dtype)
    return placed.at[:, target].set(part, mode="drop")


def shards(parent_front, child_blocks, row_maps, front_size):
    rows, width = parent_front.shape
    half = child_blocks.shape[1] // 2
    side = lax.axis_index("cube")
    front_pos = lax.axis_index("front")
    row_start = lax.axis_index(("cube", "front")) * rows
    col_start = lax.axis_index("col") * width
    row_ids = row_start + jnp.arange(rows, dtype=jnp.int32)
    col_ids = col_start + jnp.arange(width, dtype=jnp.int32)
    own_map = lax.dynamic_index_in_dim(row_maps, side, 0, keepdims=False)
    other_map = lax.dynamic_index_in_dim(row_maps, 1 - side, 0, keepdims=False)
    first = front_pos * 2 * half + side * half
    own_rows = lax.dynamic_slice_in_dim(own_map, first, half) - row_start
    other_rows = lax.dynamic_slice_in_dim(other_map, first, half) - row_start
    local_block = child_blocks[0]
    kept_rows = lax.dynamic_slice_in_dim(local_block, side * half, half, 0)
    sent_rows = lax.dynamic_slice_in_dim(local_block, (1 - side) * half, half, 0)
    kept = place_columns(kept_rows, own_map, col_start, width)
    arrived = swapped(sent_rows, "cube", 0)
    incoming = place_columns(arrived, other_map, col_start, width)
    matrix = parent_front.at[own_rows].add(kept.astype(jnp.float32))
    matrix = matrix.at[other_rows].add(incoming.astype(jnp.float32))
    live_rows = row_ids < front_size[0]
    live_cols = col_ids < front_size[0]
    matrix = jnp.where(live_rows[:, None] & live_cols[None, :], matrix, 0.0)
    matrix = matrix + jnp.where(
        (row_ids[:, None] == col_ids[None, :]) & jnp.logical_not(live_rows)[:, None], 1.0, 0.0
    )
    groups = lax.axis_size(("cube", "front")) // lax.axis_size("col")
    panels = []
    for index in range(NP):
        lower = index * PW
        root = lower // rows
        offset = lower % rows
        column_piece = spread(matrix[:, lower : lower + PW], "col", 0)
        diagonal = spread(column_piece, ("cube", "front"), root)
        diag_factor = jnp.linalg.cholesky(diagonal)
        panel = lax.linalg.triangular_solve(
            diag_factor, column_piece, left_side=False, lower=True, transpose_a=True
        )
        panel = jnp.where(row_ids[:, None] >= lower, panel, 0.0)
        column_block = lax.axis_index("col")

        def collect(turn, buffer):
            piece = spread(panel, ("cube", "front"), column_block * groups + turn)
            return lax.dynamic_update_slice_in_dim(buffer, piece, turn * rows, 0)

        transposed = lax.fori_loop(0, groups, collect, jnp.zeros((width, PW), jnp.float32))
        update = lax.dot_general(
            panel, transposed, (((1,), (1,)), ((), ())), precision=lax.Precision.HIGHEST
        )
        matrix = matrix - update
        panels.append(panel)
    factor = jnp.concatenate(panels, axis=1)
    keep_rows = row_ids >= K
    keep_cols = col_ids >= K
    schur = jnp.where(keep_rows[:, None] & keep_cols[None, :], matrix, 0.0)
    return (factor, schur)


def solution(mesh):
    in_specs = (P(("cube", "front"), "col"), P("cube", "front", None), P(), P())
    out_specs = (P(("cube", "front"), None), P(("cube", "front"), "col"))
    return jax.shard_map(shards, mesh=mesh, in_specs=in_specs, out_specs=out_specs, check_vma=False)
```

profile of v0, /device:TPU:1, one launch (start us, length us, event | category | flops | bytes accessed | tf_op | source)
XLA Modules:
  0.0 2287.5 jit_solution(12870926915053730180)
XLA Ops:
  18.1 27.1 %scatter_custom_fusion = bf16[192,2048]{0,1:T(8,128)(2,1)S(1)} fusion(s32[6144]{0:T(1024)S(1)} %bitcast.93, bf16[6144,192]{1,0:T(8,128)(2,1)} %copy.29, bf16[]{:T(256)} %constant.328.clone.1), kind=kCustom, calls=%fused_computation.29 | custom fusion | bytes 786944 | tf_op jit(solution)/shard_map/scatter | solution.py:25
  70.7 27.0 %scatter_custom_fusion.2 = bf16[192,2048]{0,1:T(8,128)(2,1)S(1)} fusion(s32[6144]{0:T(1024)S(1)} %bitcast.92, bf16[6144,192]{1,0:T(8,128)(2,1)} %copy.31, bf16[]{:T(256)} %constant.328.clone.1), kind=kCustom, calls=%fused_computation.27 | custom fusion | bytes 786944 | tf_op jit(solution)/shard_map/scatter | solution.py:25
  109.3 43.3 %all-reduce.8.cloned.1.call-done = f32[256,256]{0,1:T(8,128)} async-done(((f32[256,256]{0,1:T(8,128)}), f32[256,256]{0,1:T(8,128)}) %all-reduce.8.cloned.1.call-update) | async-done | bytes 262160 | tf_op jit(solution)/shard_map/psum | solution.py:17
  153.4 107.6 %all-reduce.10.cloned.1.call-done = f32[256,256]{0,1:T(8,128)} async-done(((f32[256,256]{0,1:T(8,128)}), f32[256,256]{0,1:T(8,128)}) %all-reduce.10.cloned.1.call-update) | async-done | bytes 262160 | tf_op jit(solution)/shard_map/psum | solution.py:17
  325.4 863.9 %while.34 = (s32[]{:T(128)}, f32[2048,256]{1,0:T(8,128)}, s32[]{:T(128)}, f32[256,256]{1,0:T(8,128)S(1)}, s32[]{:T(128)}, /*index=5*/u32[]{:T(128)}, u32[]{:T(12...) while((s32[]{:T(128)}, f32[2048,256]{1,0:T(8,128)}, s32[]{:T(128)}, ...), condition=%wide.region_12.15_spmd, body=%wide.region_10.14_spmd.sunk | while | flops 131088 | bytes 2621765 | solution.py:75
  326.2 105.7 %all-reduce.16.cloned.1.call-done = f32[256,256]{1,0:T(8,128)} async-done(((f32[256,256]{1,0:T(8,128)}), f32[256,256]{1,0:T(8,128)}) %all-reduce.16.cloned.1.call-update) | async-done | bytes 262160 | tf_op jit(solution)/shard_map/while/body/eval_jaxpr/psum | solution.py:17
  434.3 105.4 %all-reduce.16.cloned.1.call-done = f32[256,256]{1,0:T(8,128)} async-done(((f32[256,256]{1,0:T(8,128)}), f32[256,256]{1,0:T(8,128)}) %all-reduce.16.cloned.1.call-update) | async-done | bytes 262160 | tf_op jit(solution)/shard_map/while/body/eval_jaxpr/psum | solution.py:17
  542.1 105.4 %all-reduce.16.cloned.1.call-done = f32[256,256]{1,0:T(8,128)} async-done(((f32[256,256]{1,0:T(8,128)}), f32[256,256]{1,0:T(8,128)}) %all-reduce.16.cloned.1.call-update) | async-done | bytes 262160 | tf_op jit(solution)/shard_map/while/body/eval_jaxpr/psum | solution.py:17
  650.0 105.4 %all-reduce.16.cloned.1.call-done = f32[256,256]{1,0:T(8,128)} async-done(((f32[256,256]{1,0:T(8,128)}), f32[256,256]{1,0:T(8,128)}) %all-reduce.16.cloned.1.call-update) | async-done | bytes 262160 | tf_op jit(solution)/shard_map/while/body/eval_jaxpr/psum | solution.py:17
  757.8 105.7 %all-reduce.16.cloned.1.call-done = f32[256,256]{1,0:T(8,128)} async-done(((f32[256,256]{1,0:T(8,128)}), f32[256,256]{1,0:T(8,128)}) %all-reduce.16.cloned.1.call-update) | async-done | bytes 262160 | tf_op jit(solution)/shard_map/while/body/eval_jaxpr/psum | solution.py:17
  866.0 105.7 %all-reduce.16.cloned.1.call-done = f32[256,256]{1,0:T(8,128)} async-done(((f32[256,256]{1,0:T(8,128)}), f32[256,256]{1,0:T(8,128)}) %all-reduce.16.cloned.1.call-update) | async-done | bytes 262160 | tf_op jit(solution)/shard_map/while/body/eval_jaxpr/psum | solution.py:17
  974.1 105.7 %all-reduce.16.cloned.1.call-done = f32[256,256]{1,0:T(8,128)} async-done(((f32[256,256]{1,0:T(8,128)}), f32[256,256]{1,0:T(8,128)}) %all-reduce.16.cloned.1.call-update) | async-done | bytes 262160 | tf_op jit(solution)/shard_map/while/body/eval_jaxpr/psum | solution.py:17
  1082.2 105.4 %all-reduce.16.cloned.1.call-done = f32[256,256]{1,0:T(8,128)} async-done(((f32[256,256]{1,0:T(8,128)}), f32[256,256]{1,0:T(8,128)}) %all-reduce.16.cloned.1.call-update) | async-done | bytes 262160 | tf_op jit(solution)/shard_map/while/body/eval_jaxpr/psum | solution.py:17
  1195.0 39.8 %all-reduce.12.cloned.1.call-done = f32[256,256]{0,1:T(8,128)} async-done(((f32[256,256]{0,1:T(8,128)}), f32[256,256]{0,1:T(8,128)}) %all-reduce.12.cloned.1.call-update) | async-done | bytes 262160 | tf_op jit(solution)/shard_map/psum | solution.py:17
  1236.5 106.5 %all-reduce.14.cloned.1.call-done = f32[256,256]{0,1:T(8,128)} async-done(((f32[256,256]{0,1:T(8,128)}), f32[256,256]{0,1:T(8,128)}) %all-reduce.14.cloned.1.call-update) | async-done | bytes 262160 | tf_op jit(solution)/shard_map/psum | solution.py:17
  1408.1 863.3 %while.35 = (s32[]{:T(128)}, f32[2048,256]{1,0:T(8,128)}, s32[]{:T(128)}, f32[256,256]{1,0:T(8,128)S(1)}, s32[]{:T(128)}, /*index=5*/u32[]{:T(128)}, u32[]{:T(12...) while((s32[]{:T(128)}, f32[2048,256]{1,0:T(8,128)}, s32[]{:T(128)}, ...), condition=%wide.region_17.20_spmd, body=%wide.region_15.19_spmd.sunk | while | flops 131088 | bytes 2621765 | solution.py:75
  1408.9 105.7 %all-reduce.18.cloned.1.call-done = f32[256,256]{1,0:T(8,128)} async-done(((f32[256,256]{1,0:T(8,128)}), f32[256,256]{1,0:T(8,128)}) %all-reduce.18.cloned.1.call-update) | async-done | bytes 262160 | tf_op jit(solution)/shard_map/while/body/eval_jaxpr/psum | solution.py:17
  1517.1 105.4 %all-reduce.18.cloned.1.call-done = f32[256,256]{1,0:T(8,128)} async-done(((f32[256,256]{1,0:T(8,128)}), f32[256,256]{1,0:T(8,128)}) %all-reduce.18.cloned.1.call-update) | async-done | bytes 262160 | tf_op jit(solution)/shard_map/while/body/eval_jaxpr/psum | solution.py:17
  1624.9 105.4 %all-reduce.18.cloned.1.call-done = f32[256,256]{1,0:T(8,128)} async-done(((f32[256,256]{1,0:T(8,128)}), f32[256,256]{1,0:T(8,128)}) %all-reduce.18.cloned.1.call-update) | async-done | bytes 262160 | tf_op jit(solution)/shard_map/while/body/eval_jaxpr/psum | solution.py:17
  1732.7 105.4 %all-reduce.18.cloned.1.call-done = f32[256,256]{1,0:T(8,128)} async-done(((f32[256,256]{1,0:T(8,128)}), f32[256,256]{1,0:T(8,128)}) %all-reduce.18.cloned.1.call-update) | async-done | bytes 262160 | tf_op jit(solution)/shard_map/while/body/eval_jaxpr/psum | solution.py:17
  1840.5 105.4 %all-reduce.18.cloned.1.call-done = f32[256,256]{1,0:T(8,128)} async-done(((f32[256,256]{1,0:T(8,128)}), f32[256,256]{1,0:T(8,128)}) %all-reduce.18.cloned.1.call-update) | async-done | bytes 262160 | tf_op jit(solution)/shard_map/while/body/eval_jaxpr/psum | solution.py:17
  1948.4 105.4 %all-reduce.18.cloned.1.call-done = f32[256,256]{1,0:T(8,128)} async-done(((f32[256,256]{1,0:T(8,128)}), f32[256,256]{1,0:T(8,128)}) %all-reduce.18.cloned.1.call-update) | async-done | bytes 262160 | tf_op jit(solution)/shard_map/while/body/eval_jaxpr/psum | solution.py:17
  2056.2 105.7 %all-reduce.18.cloned.1.call-done = f32[256,256]{1,0:T(8,128)} async-done(((f32[256,256]{1,0:T(8,128)}), f32[256,256]{1,0:T(8,128)}) %all-reduce.18.cloned.1.call-update) | async-done | bytes 262160 | tf_op jit(solution)/shard_map/while/body/eval_jaxpr/psum | solution.py:17
  2164.4 105.4 %all-reduce.18.cloned.1.call-done = f32[256,256]{1,0:T(8,128)} async-done(((f32[256,256]{1,0:T(8,128)}), f32[256,256]{1,0:T(8,128)}) %all-reduce.18.cloned.1.call-update) | async-done | bytes 262160 | tf_op jit(solution)/shard_map/while/body/eval_jaxpr/psum | solution.py:17
  (173 shorter events, 237.2 us)
Async XLA Ops:
  7.2 145.5 %all-reduce.8.cloned.1.call-start = ((), (), s32[]{:S(2)}) async-start(), calls=%async_computation | async-start | bytes 524288 | tf_op jit(solution)/shard_map/psum | solution.py:17
  11.4 54.8 %collective-permute-start = (bf16[192,6144]{1,0:T(8,128)(2,1)}, bf16[192,6144]{1,0:T(8,128)(2,1)}, u32[]{:S(2)}, u32[]{:S(2)}) collective-permute-start(bf16[192,6144]{1,0:T(8,128)(2,1)} %get-tuple-element.304), channel_id=1, source_target_pairs={{0,64},{64,0},{1,65},{65,1},{2,66},{66,2},{3,67},{67,3},{4,68},{68... | collective-permute-start | bytes 7077896 | tf_op jit(solution)/shard_map/ppermute | solution.py:12
  109.2 151.7 %all-reduce.10.cloned.1.call-start = ((), (), s32[]{:S(2)}) async-start(), calls=%async_computation.1 | async-start | bytes 524288 | tf_op jit(solution)/shard_map/psum | solution.py:17
  153.4 169.5 %copy-start.3 = (f32[256,256]{0,1:T(8,128)S(1)}, f32[256,256]{0,1:T(8,128)}, u32[]{:S(2)}) copy-start(f32[256,256]{0,1:T(8,128)} %all-reduce.8.cloned.1.call-done) | copy-start | bytes 786436
  325.4 106.5 %all-reduce.16.cloned.1.call-start = ((), (), s32[]{:S(2)}) async-start(), calls=%async_computation.4 | async-start | bytes 524288 | tf_op jit(solution)/shard_map/while/body/eval_jaxpr/psum | solution.py:17
  433.6 106.2 %all-reduce.16.cloned.1.call-start = ((), (), s32[]{:S(2)}) async-start(), calls=%async_computation.4 | async-start | bytes 524288 | tf_op jit(solution)/shard_map/while/body/eval_jaxpr/psum | solution.py:17
  541.4 106.2 %all-reduce.16.cloned.1.call-start = ((), (), s32[]{:S(2)}) async-start(), calls=%async_computation.4 | async-start | bytes 524288 | tf_op jit(solution)/shard_map/while/body/eval_jaxpr/psum | solution.py:17
  649.2 106.2 %all-reduce.16.cloned.1.call-start = ((), (), s32[]{:S(2)}) async-start(), calls=%async_computation.4 | async-start | bytes 524288 | tf_op jit(solution)/shard_map/while/body/eval_jaxpr/psum | solution.py:17
  757.0 106.5 %all-reduce.16.cloned.1.call-start = ((), (), s32[]{:S(2)}) async-start(), calls=%async_computation.4 | async-start | bytes 524288 | tf_op jit(solution)/shard_map/while/body/eval_jaxpr/psum | solution.py:17
  865.2 106.5 %all-reduce.16.cloned.1.call-start = ((), (), s32[]{:S(2)}) async-start(), calls=%async_computation.4 | async-start | bytes 524288 | tf_op jit(solution)/shard_map/while/body/eval_jaxpr/psum | solution.py:17
  973.3 106.5 %all-reduce.16.cloned.1.call-start = ((), (), s32[]{:S(2)}) async-start(), calls=%async_computation.4 | async-start | bytes 524288 | tf_op jit(solution)/shard_map/while/body/eval_jaxpr/psum | solution.py:17
  1081.5 106.2 %all-reduce.16.cloned.1.call-start = ((), (), s32[]{:S(2)}) async-start(), calls=%async_computation.4 | async-start | bytes 524288 | tf_op jit(solution)/shard_map/while/body/eval_jaxpr/psum | solution.py:17
  1189.3 45.5 %all-reduce.12.cloned.1.call-start = ((), (), s32[]{:S(2)}) async-start(), calls=%async_computation.2 | async-start | bytes 524288 | tf_op jit(solution)/shard_map/psum | solution.py:17
  1194.9 148.1 %all-reduce.14.cloned.1.call-start = ((), (), s32[]{:S(2)}) async-start(), calls=%async_computation.3 | async-start | bytes 524288 | tf_op jit(solution)/shard_map/psum | solution.py:17
  1236.5 169.0 %copy-start.4 = (f32[256,256]{0,1:T(8,128)S(1)}, f32[256,256]{0,1:T(8,128)}, u32[]{:S(2)}) copy-start(f32[256,256]{0,1:T(8,128)} %all-reduce.12.cloned.1.call-done) | copy-start | bytes 786436
  1406.6 864.9 %copy-start.1 = (f32[256,2048]{0,1:T(8,128)S(1)}, f32[256,2048]{0,1:T(8,128)}, u32[]{:S(2)}) copy-start(f32[256,2048]{0,1:T(8,128)} %copy-done) | copy-start | bytes 6291460
  1408.1 106.5 %all-reduce.18.cloned.1.call-start = ((), (), s32[]{:S(2)}) async-start(), calls=%async_computation.5 | async-start | bytes 524288 | tf_op jit(solution)/shard_map/while/body/eval_jaxpr/psum | solution.py:17
  1516.3 106.2 %all-reduce.18.cloned.1.call-start = ((), (), s32[]{:S(2)}) async-start(), calls=%async_computation.5 | async-start | bytes 524288 | tf_op jit(solution)/shard_map/while/body/eval_jaxpr/psum | solution.py:17
  1624.1 106.2 %all-reduce.18.cloned.1.call-start = ((), (), s32[]{:S(2)}) async-start(), calls=%async_computation.5 | async-start | bytes 524288 | tf_op jit(solution)/shard_map/while/body/eval_jaxpr/psum | solution.py:17
  1732.0 106.2 %all-reduce.18.cloned.1.call-start = ((), (), s32[]{:S(2)}) async-start(), calls=%async_computation.5 | async-start | bytes 524288 | tf_op jit(solution)/shard_map/while/body/eval_jaxpr/psum | solution.py:17
  1839.8 106.2 %all-reduce.18.cloned.1.call-start = ((), (), s32[]{:S(2)}) async-start(), calls=%async_computation.5 | async-start | bytes 524288 | tf_op jit(solution)/shard_map/while/body/eval_jaxpr/psum | solution.py:17
  1947.6 106.2 %all-reduce.18.cloned.1.call-start = ((), (), s32[]{:S(2)}) async-start(), calls=%async_computation.5 | async-start | bytes 524288 | tf_op jit(solution)/shard_map/while/body/eval_jaxpr/psum | solution.py:17
  2055.5 106.5 %all-reduce.18.cloned.1.call-start = ((), (), s32[]{:S(2)}) async-start(), calls=%async_computation.5 | async-start | bytes 524288 | tf_op jit(solution)/shard_map/while/body/eval_jaxpr/psum | solution.py:17
  2163.6 106.2 %all-reduce.18.cloned.1.call-start = ((), (), s32[]{:S(2)}) async-start(), calls=%async_computation.5 | async-start | bytes 524288 | tf_op jit(solution)/shard_map/while/body/eval_jaxpr/psum | solution.py:17
  (3 other events, 33.3 us)
Sparse Core Ops, SparseCore 0:
  109.4 43.2 all-reduce.7
  156.4 104.5 all-reduce.9
  330.0 101.8 all-reduce.15
  437.8 101.8 all-reduce.15
  545.7 101.8 all-reduce.15
  653.5 101.8 all-reduce.15
  761.6 101.8 all-reduce.15
  869.8 101.8 all-reduce.15
  977.9 101.8 all-reduce.15
  1085.8 101.8 all-reduce.15
  1195.0 39.7 all-reduce.11
  1238.5 104.5 all-reduce.13
  1412.7 101.8 all-reduce.17
  1520.6 101.8 all-reduce.17
  1628.4 101.8 all-reduce.17
  1736.2 101.8 all-reduce.17
  1844.1 101.8 all-reduce.17
  1951.9 101.8 all-reduce.17
  2060.1 101.8 all-reduce.17
  2167.9 101.8 all-reduce.17
where the time goes:
time: 2300 us; the launch traced here: 2290 us
  waiting for transfers between devices  2000 us (87%)
  other arithmetic  138 us (6%)
  local copies, waits for them, and re-layouts  115 us (5%)
    psum x20, waiting for transfers between devices, spread(): return lax.psum(block, axis)  1990 us
    another operation x13, other arithmetic, shards(): diag_factor = jnp.linalg.cholesky(diagonal)  68.6 us
    scatter x4, local copies, waits for them, and re-layouts, place_columns(): return placed.at[:, target].set(part, mode='drop')  56.5 us
  transfers between devices with their start and end apart: 21, of which 21 were waited for; matrix products, arithmetic and copies ran while one was open for 2% of the time, Pallas kernels for 0%

commit v1 on v0

v1 whole, which is shorter than its diff:
```python
import jax
import jax.numpy as jnp
from jax import lax
from jax.sharding import PartitionSpec as P

PW = 256
NP = 2
K = 512

HI = lax.Precision.HIGHEST


def swapped(shard, axis, distance):
    return lax.ppermute(shard, axis, [(i, i ^ 1 << distance) for i in range(lax.axis_size(axis))])


def spread(block, axis, owner):
    block = jnp.where(lax.axis_index(axis) == owner, block, jnp.zeros_like(block))
    return lax.psum(block, axis)


def pick_columns(block, col, nb, grp):
    n = block.shape[0]
    halves = block.shape[-1] // (2 * grp)
    shaped = block.reshape(n, halves, 2, grp)
    start = (col * nb) % halves
    parity = (col * nb) // halves
    shaped = lax.dynamic_slice_in_dim(shaped, start, nb, 1)
    shaped = lax.dynamic_index_in_dim(shaped, parity, 2, keepdims=False)
    return shaped


def extend(part, row_local, col_local, rows, blk):
    n, nb, grp = part.shape
    pr = (jnp.arange(rows, dtype=jnp.int32)[:, None] == row_local[None, :]).astype(part.dtype)
    pc = (col_local[:, :, None] == jnp.arange(blk, dtype=jnp.int32)[None, None, :]).astype(part.dtype)
    placed_rows = jnp.dot(pr, part.reshape(n, nb * grp), preferred_element_type=jnp.float32)
    placed_rows = placed_rows.astype(part.dtype).reshape(rows, nb, grp)
    placed = jnp.einsum("ija,jab->ijb", placed_rows, pc, preferred_element_type=jnp.float32)
    return placed.reshape(rows, nb * blk)


def shards(parent_front, child_blocks, row_maps, front_size):
    rows, width = parent_front.shape
    half = child_blocks.shape[1] // 2
    grp = half
    blk = rows
    nb = width // blk
    side = lax.axis_index("cube")
    front_pos = lax.axis_index("front")
    col = lax.axis_index("col")
    row_block = lax.axis_index(("cube", "front"))
    row_start = row_block * rows
    col_start = col * width
    row_ids = row_start + jnp.arange(rows, dtype=jnp.int32)
    col_ids = col_start + jnp.arange(width, dtype=jnp.int32)

    own_map = lax.dynamic_index_in_dim(row_maps, side, 0, keepdims=False)
    other_map = lax.dynamic_index_in_dim(row_maps, 1 - side, 0, keepdims=False)
    first = front_pos * 2 * half + side * half
    own_rows = lax.dynamic_slice_in_dim(own_map, first, half) - row_start
    other_rows = lax.dynamic_slice_in_dim(other_map, first, half) - row_start
    blk_starts = col_start + blk * jnp.arange(nb, dtype=jnp.int32)[:, None]
    own_cols = pick_columns(own_map[None], col, nb, grp)[0] - blk_starts
    other_cols = pick_columns(other_map[None], col, nb, grp)[0] - blk_starts

    local_block = child_blocks[0]
    kept_rows = lax.dynamic_slice_in_dim(local_block, side * half, half, 0)
    sent_rows = lax.dynamic_slice_in_dim(local_block, (1 - side) * half, half, 0)
    kept = pick_columns(kept_rows, col, nb, grp)
    sent = pick_columns(sent_rows, col, nb, grp)
    arrived = swapped(sent, "cube", 0)
    own_part = extend(kept, own_rows, own_cols, rows, blk)
    other_part = extend(arrived, other_rows, other_cols, rows, blk)
    first_child = jnp.where(side == 0, own_part, other_part)
    second_child = jnp.where(side == 0, other_part, own_part)
    matrix = parent_front + first_child
    matrix = matrix + second_child

    live_rows = row_ids < front_size[0]
    live_cols = col_ids < front_size[0]
    matrix = jnp.where(live_rows[:, None] & live_cols[None, :], matrix, 0.0)
    matrix = matrix + jnp.where(
        (row_ids[:, None] == col_ids[None, :]) & jnp.logical_not(live_rows)[:, None], 1.0, 0.0
    )

    pcols = NP * PW
    nd = pcols // rows
    head_local = matrix[:, :pcols]
    own = spread(head_local, "col", 0)
    top_parts = jnp.where(
        (jnp.arange(nd)[:, None, None] == row_block) & (col == 0), head_local[None], 0.0
    )
    top = lax.psum(top_parts, ("cube", "front", "col")).reshape(pcols, pcols)
    top_ids = jnp.arange(pcols, dtype=jnp.int32)

    panels = []
    for index in range(NP):
        lower = index * PW
        diag_factor = jnp.linalg.cholesky(top[lower : lower + PW, lower : lower + PW])
        both = jnp.concatenate([top[:, lower : lower + PW], own[:, lower : lower + PW]], 0)
        solved = lax.linalg.triangular_solve(
            diag_factor, both, left_side=False, lower=True, transpose_a=True
        )
        top_panel = jnp.where((top_ids >= lower)[:, None], solved[:pcols], 0.0)
        panel = jnp.where((row_ids >= lower)[:, None], solved[pcols:], 0.0)
        if index + 1 < NP:
            top = top - jnp.dot(top_panel, top_panel.T, precision=HI)
            own = own - jnp.dot(panel, top_panel.T, precision=HI)
        panels.append(panel)
    factor = jnp.concatenate(panels, axis=1)

    gathered = lax.all_gather(factor, ("cube", "front"), tiled=True)
    col_factor = lax.dynamic_slice_in_dim(gathered, col_start, width, 0)
    update = lax.dot_general(
        factor, col_factor, (((1,), (1,)), ((), ())), precision=HI
    )
    matrix = matrix - update
    keep_rows = row_ids >= K
    keep_cols = col_ids >= K
    schur = jnp.where(keep_rows[:, None] & keep_cols[None, :], matrix, 0.0)
    return (factor, schur)


def solution(mesh):
    in_specs = (P(("cube", "front"), "col"), P("cube", "front", None), P(), P())
    out_specs = (P(("cube", "front"), None), P(("cube", "front"), "col"))
    return jax.shard_map(shards, mesh=mesh, in_specs=in_specs, out_specs=out_specs, check_vma=False)
```

time: 2300 us -> 449 us (0.20)
  waiting for transfers between devices: 2000 us -> 230 us
  local copies, waits for them, and re-layouts: 115 us -> 53.3 us
    psum x20 -> x1, waiting for transfers between devices: 1990 us -> 0.02 us  [spread(): return lax.psum(block, axis)]
    psum x0 -> x1, waiting for transfers between devices: none -> 150 us  [shards(): top = lax.psum(top_parts, ('cube', 'front', 'col')).reshape(pcols, pcols)]
    all_gather x0 -> x1, waiting for transfers between devices: none -> 76.8 us  [shards(): gathered = lax.all_gather(factor, ('cube', 'front'), tiled=True)]
    scatter x4 -> x0, local copies, waits for them, and re-layouts: 56.5 us -> none  [place_columns(): return placed.at[:, target].set(part, mode='drop')]
    dynamic_update_slice x16 -> x0, local copies, waits for them, and re-layouts: 26.7 us -> none  [collect(): return lax.dynamic_update_slice_in_dim(buffer, piece, turn * rows, 0)]
    another operation x18 -> x19, other arithmetic: 108 us -> 109 us  [the longest x14 69.5 us: shards(): diag_factor = jnp.linalg.cholesky(top[lower:lower + PW, lower:lower + PW])]
  transfers between devices with their start and end apart: 21 -> 4, of which waited for: 21 -> 3; matrix products, arithmetic and copies ran while one was open for 2% -> 18% of each run, Pallas kernels for 0% -> 0%
where the time goes in v1:
time: 449 us; the launch traced here: 444 us
  waiting for transfers between devices  230 us (51%)
  other arithmetic  117 us (26%)
  local copies, waits for them, and re-layouts  53.3 us (12%)
  matrix products  22.4 us (5%)
  between operations  17.8 us (4%)
    psum x1, waiting for transfers between devices, shards(): top = lax.psum(top_parts, ('cube', 'front', 'col')).reshape(pcols, pcols)  150 us
    all_gather x1, waiting for transfers between devices, shards(): gathered = lax.all_gather(factor, ('cube', 'front'), tiled=True)  76.8 us
    another operation x14, other arithmetic, shards(): diag_factor = jnp.linalg.cholesky(top[lower:lower + PW, lower:lower + PW])  69.5 us
    another operation x5, other arithmetic, shards(): lax.linalg.triangular_solve(diag_factor, both, left_side=False, lower=Tru...  39.6 us
    reshape x2, local copies, waits for them, and re-layouts, pick_columns(): shaped = block.reshape(n, halves, 2, grp)  13.8 us
    unnamed x17, local copies, waits for them, and re-layouts  10.8 us
    dot_general x1, matrix products, shards(): lax.dot_general(factor, col_factor, (((1,), (1,)), ((), ())), precision=HI)  10.6 us
    dynamic_slice x3, local copies, waits for them, and re-layouts, pick_columns(): shaped = lax.dynamic_index_in_dim(shaped, parity, 2, keepdims=False)  9.68 us
  transfers between devices with their start and end apart: 4, of which 3 were waited for; matrix products, arithmetic and copies ran while one was open for 18% of the time, Pallas kernels for 0%

profile of v1, /device:TPU:1, one launch (start us, length us, event | category | flops | bytes accessed | tf_op | source)
XLA Modules:
  0.0 444.0 jit_solution(3446853785531009642)
XLA Ops:
  7.2 4.2 constant_dynamic-slice_fusion.5
  11.5 9.0 %reshape.144 = bf16[192,16,2,192]{3,2,1,0:T(2,128)(2,1)} reshape(bf16[1,192,6144]{2,1,0:T(8,128)(2,1)} %get-tuple-element.51) | data formatting | bytes 4718592 | tf_op jit(solution)/shard_map/reshape | solution.py:25
  20.5 3.1 constant_dynamic-slice_fusion.2
  24.6 3.9 collective-permute-start
  29.2 4.8 %reshape.141 = bf16[192,16,2,192]{3,2,1,0:T(2,128)(2,1)} reshape(bf16[1,192,6144]{2,1,0:T(8,128)(2,1)S(1)} %get-tuple-element.50) | data formatting | bytes 4718592 | tf_op jit(solution)/shard_map/reshape | solution.py:25
  34.0 6.6 %dynamic-slice_reduce_fusion = bf16[192,8,192]{2,1,0:T(8,128)(2,1)S(1)} fusion(bf16[192,16,2,192]{3,2,1,0:T(2,128)(2,1)} %reshape.141, s32[]{:T(128)S(6)} %select_n.127, s32[]{:T(128)S(6)} %select_n.130), kind=kLoop, calls=%fused_computation.15 | loop fusion | bytes 1179656 | tf_op jit(solution)/shard_map/jit(dynamic_index_in_dim)/dynamic_slice | solution.py:29
  42.1 1.8 copy.28
  45.8 1.8 reshape.145
  51.1 2.0 fusion.9
  56.8 150.5 %all-reduce.4.cloned.1.call-done = f32[512,512]{0,1:T(8,128)} async-done(((f32[512,512]{0,1:T(8,128)}), f32[512,512]{0,1:T(8,128)}) %all-reduce.4.cloned.1.call-update) | async-done | bytes 1048592 | tf_op jit(solution)/shard_map/psum | solution.py:94
  209.3 11.7 %cholesky.130 = f32[128,128]{1,0:T(8,128)S(1)} custom-call(f32[128,128]{1,0:T(8,128)S(1)} %cholesky.194), custom_call_target="Cholesky" | custom-call | tf_op jit(solution)/shard_map/jit(cholesky)/cholesky | solution.py:100
  221.7 9.8 %custom-call.13 = f32[1,128,128]{1,2,0:T(8,128)S(1)} custom-call(f32[1,128,128]{2,1,0:T(8,128)S(1)} %get-tuple-element.63), custom_call_target="InvertDiagBlocksLowerTriangular" | custom-call | tf_op jit(solution)/shard_map/jit(cholesky)/cholesky | solution.py:100
  232.0 11.7 %cholesky.147 = f32[128,128]{1,0:T(8,128)S(1)} custom-call(f32[128,128]{1,0:T(8,128)S(1)} %convolution_subtract_fusion.4), custom_call_target="Cholesky" | custom-call | tf_op jit(solution)/shard_map/jit(cholesky)/cholesky | solution.py:100
  245.9 4.0 while.4
  249.9 19.8 %custom-call.14 = f32[2,128,128]{1,2,0:T(8,128)S(1)} custom-call(f32[2,128,128]{2,1,0:T(8,128)S(1)} %get-tuple-element.18), custom_call_target="InvertDiagBlocksLowerTriangular" | custom-call | tf_op jit(solution)/shard_map/triangular_solve/custom-call.0 | solution.py:102
  279.1 11.7 %cholesky.164 = f32[128,128]{1,0:T(8,128)S(1)} custom-call(f32[128,128]{1,0:T(8,128)S(1)} %cholesky.197), custom_call_target="Cholesky" | custom-call | tf_op jit(solution)/shard_map/jit(cholesky)/cholesky | solution.py:100
  291.6 9.8 %custom-call.15 = f32[1,128,128]{1,2,0:T(8,128)S(1)} custom-call(f32[1,128,128]{2,1,0:T(8,128)S(1)} %get-tuple-element.59), custom_call_target="InvertDiagBlocksLowerTriangular" | custom-call | tf_op jit(solution)/shard_map/jit(cholesky)/cholesky | solution.py:100
  303.6 11.9 %cholesky.181 = f32[128,128]{1,0:T(8,128)S(1)} custom-call(f32[128,128]{1,0:T(8,128)S(1)} %convolution_subtract_fusion.3), custom_call_target="Cholesky" | custom-call | tf_op jit(solution)/shard_map/jit(cholesky)/cholesky | solution.py:100
  317.6 4.1 while.5
  321.7 19.7 %custom-call.16 = f32[2,128,128]{1,2,0:T(8,128)S(1)} custom-call(f32[2,128,128]{2,1,0:T(8,128)S(1)} %get-tuple-element.19), custom_call_target="InvertDiagBlocksLowerTriangular" | custom-call | tf_op jit(solution)/shard_map/triangular_solve/custom-call.0 | solution.py:102
  344.9 2.0 copy.36
  346.9 76.8 %all-gather.2.cloned.1.call-done = f32[8192,512]{0,1:T(8,128)} async-done(((f32[256,512]{0,1:T(8,128)}), f32[8192,512]{0,1:T(8,128)}) %all-gather.2.cloned.1.call-update) | async-done | bytes 16777232 | tf_op jit(solution)/shard_map/all_gather | solution.py:113
  423.8 10.6 %fusion.5 = f32[256,2048]{0,1:T(8,128)} fusion(f32[256,2048]{0,1:T(8,128)S(1)} %fusion.9, f32[8192,512]{0,1:T(8,128)} %all-gather.2.cloned.1.call-done, s32[]{:T(128)S(6)} %select_n.151, pred[256]{0:T(512)(128)(4,1)S(1)} %fusion.39, pred[2048]{0:T(1024)(128)(4,1)S(1)} %fusion.36, f32[256,256]{0,1:T(8,128)S(1)} %fusion.21, f32[256,256]{0,1:T(8,128)S(1)} %maximum_select_fusion), kind=kOutput, calls=%fused_computation.7 | convolution fusion | flops 3222929408 | bytes 8915204 | tf_op jit(solution)/shard_map/dot_general | solution.py:115
  434.4 2.9 copy.37
  (101 shorter events, 39.9 us)
Async XLA Ops:
  7.2 200.1 %all-reduce.4.cloned.1.call-start = ((), (), s32[]{:S(2)}) async-start(), calls=%async_computation | async-start | bytes 2097152 | tf_op jit(solution)/shard_map/psum | solution.py:94
  24.6 21.2 %collective-permute-start = (bf16[192,8,192]{2,1,0:T(8,128)(2,1)}, bf16[192,8,192]{2,1,0:T(8,128)(2,1)}, u32[]{:S(2)}, u32[]{:S(2)}) collective-permute-start(bf16[192,8,192]{2,1,0:T(8,128)(2,1)} %bitcast.85), channel_id=1, source_target_pairs={{0,64},{64,0},{1,65},{65,1},{2,66},{66,2},{3,67},{67,3},{4,68},{68... | collective-permute-start | bytes 1769480 | tf_op jit(solution)/shard_map/ppermute | solution.py:14
  34.0 7.3 %copy-start.5 = (s32[2,6144]{1,0:T(2,128)S(1)}, s32[2,6144]{1,0:T(2,128)}, u32[]{:S(2)}) copy-start(s32[2,6144]{1,0:T(2,128)} %param.9) | copy-start | bytes 147460
  34.0 8.1 %copy-start.3 = (f32[256,2048]{1,0:T(8,128)S(1)}, f32[256,2048]{1,0:T(8,128)}, u32[]{:S(2)}) copy-start(f32[256,2048]{1,0:T(8,128)} %param.7) | copy-start | bytes 6291460
  49.5 1.6 copy-start
  55.5 215.3 %all-reduce.6.cloned.1.call-start = ((), (), s32[]{:S(2)}) async-start(), calls=%async_computation.1 | async-start | bytes 1048576 | tf_op jit(solution)/shard_map/psum | solution.py:19
  56.3 367.5 %all-gather.2.cloned.1.call-start = ((), (), s32[]{:S(2)}) async-start(), calls=%async_computation.2 | async-start | bytes 17301504 | tf_op jit(solution)/shard_map/all_gather | solution.py:113
  272.8 2.4 copy-start.2
  276.3 1.0 copy-start.1
  278.4 0.7 copy-start.4
Sparse Core Ops, SparseCore 0:
  55.7 151.5 all-reduce.3
  210.1 40.0 all-reduce.5
  345.0 78.7 all-gather.1

commit v2 on v1

--- a/solution.py
+++ b/solution.py
@@ -85,36 +85,61 @@
     )
 
     pcols = NP * PW
+    head_local = matrix[:, :pcols]
+    ncol = lax.axis_size("col")
+    arrived_heads = [
+        lax.ppermute(head_local, "col", [(0, d)]) for d in range(1, ncol)
+    ]
+    own = head_local
+    for d, piece in enumerate(arrived_heads, start=1):
+        own = jnp.where(col == d, piece, own)
+
+    everyone = ("cube", "front", "col")
+    ndev = lax.axis_size(everyone)
     nd = pcols // rows
-    head_local = matrix[:, :pcols]
-    own = spread(head_local, "col", 0)
-    top_parts = jnp.where(
-        (jnp.arange(nd)[:, None, None] == row_block) & (col == 0), head_local[None], 0.0
+    chunk = rows * pcols // ndev
+    send = jnp.concatenate(
+        [
+            jnp.where((row_block == b) & (col == 0), head_local, 0.0).reshape(ndev, chunk)
+            for b in range(nd)
+        ],
+        axis=1,
     )
-    top = lax.psum(top_parts, ("cube", "front", "col")).reshape(pcols, pcols)
+    scattered = lax.all_to_all(send, everyone, 0, 0, tiled=True)
+    src_index = [b * ncol for b in range(nd)]
+    piece = jnp.concatenate(
+        [scattered[src_index[b], b * chunk : (b + 1) * chunk] for b in range(nd)]
+    )
+    spread_out = jnp.broadcast_to(piece[None], (ndev, nd * chunk))
+    gathered_top = lax.all_to_all(spread_out, everyone, 0, 0, tiled=True)
+    top = jnp.concatenate(
+        [gathered_top[:, b * chunk : (b + 1) * chunk].reshape(rows, pcols) for b in range(nd)],
+        axis=0,
+    )
     top_ids = jnp.arange(pcols, dtype=jnp.int32)
+    eye = jnp.eye(PW, dtype=jnp.float32)
 
     panels = []
+    update = None
     for index in range(NP):
         lower = index * PW
         diag_factor = jnp.linalg.cholesky(top[lower : lower + PW, lower : lower + PW])
+        inverse = lax.linalg.triangular_solve(
+            diag_factor, eye, left_side=True, lower=True, transpose_a=False
+        )
         both = jnp.concatenate([top[:, lower : lower + PW], own[:, lower : lower + PW]], 0)
-        solved = lax.linalg.triangular_solve(
-            diag_factor, both, left_side=False, lower=True, transpose_a=True
-        )
+        solved = jnp.dot(both, inverse.T, precision=HI)
         top_panel = jnp.where((top_ids >= lower)[:, None], solved[:pcols], 0.0)
         panel = jnp.where((row_ids >= lower)[:, None], solved[pcols:], 0.0)
         if index + 1 < NP:
             top = top - jnp.dot(top_panel, top_panel.T, precision=HI)
             own = own - jnp.dot(panel, top_panel.T, precision=HI)
         panels.append(panel)
+        gathered = lax.all_gather(panel, ("cube", "front"), tiled=True)
+        col_panel = lax.dynamic_slice_in_dim(gathered, col_start, width, 0)
+        term = lax.dot_general(panel, col_panel, (((1,), (1,)), ((), ())), precision=HI)
+        update = term if update is None else update + term
     factor = jnp.concatenate(panels, axis=1)
-
-    gathered = lax.all_gather(factor, ("cube", "front"), tiled=True)
-    col_factor = lax.dynamic_slice_in_dim(gathered, col_start, width, 0)
-    update = lax.dot_general(
-        factor, col_factor, (((1,), (1,)), ((), ())), precision=HI
-    )
     matrix = matrix - update
     keep_rows = row_ids >= K
     keep_cols = col_ids >= K

time: 449 us -> 380 us (0.85)
  waiting for transfers between devices: 230 us -> 82.5 us
  blocking collectives: 0 us -> 31 us
  local copies, waits for them, and re-layouts: 53.3 us -> 71.2 us
  starting transfers between devices: 4.41 us -> 17.7 us
  matrix products: 22.4 us -> 31.4 us
  other arithmetic: 117 us -> 122 us
    psum x2 -> x0, waiting for transfers between devices: 150 us -> none  [the longest x1 150 us: shards(): top = lax.psum(top_parts, ('cube', 'front', 'col')).reshape(pcols, pcols)]
    all_to_all x0 -> x1, blocking collectives: none -> 31 us  [shards(): scattered = lax.all_to_all(send, everyone, 0, 0, tiled=True)]
    all_gather x1 -> x2, waiting for transfers between devices: 76.8 us -> 46.6 us  [shards(): gathered = lax.all_gather(panel, ('cube', 'front'), tiled=True)]
    ppermute x0 -> x3, waiting for transfers between devices: none -> 18 us  [shards(): lax.ppermute(head_local, 'col', [(0, d)])]
    all_to_all x0 -> x1, waiting for transfers between devices: none -> 17.4 us  [shards(): gathered_top = lax.all_to_all(spread_out, everyone, 0, 0, tiled=True)]
    ppermute x0 -> x3, starting transfers between devices: none -> 9.47 us  [shards(): lax.ppermute(head_local, 'col', [(0, d)])]
    dot_general x1 -> x4, matrix products: 10.6 us -> 17 us  [the longest x2 13.9 us: shards(): lax.dot_general(panel, col_panel, (((1,), (1,)), ((), ())), precision=HI)]
    reshape x0 -> x6, local copies, waits for them, and re-layouts: none -> 5.59 us  [the longest x4 3.42 us: shards(): gathered_top[:, b * chunk:(b + 1) * chunk].reshape(rows, pcols)]
  transfers between devices with their start and end apart: 4 -> 7, of which waited for: 3 -> 6; matrix products, arithmetic and copies ran while one was open for 18% -> 27% of each run, Pallas kernels for 0% -> 0%
where the time goes in v2:
time: 380 us; the launch traced here: 374 us
  other arithmetic  122 us (32%)
  waiting for transfers between devices  82.5 us (22%)
  local copies, waits for them, and re-layouts  71.2 us (19%)
  matrix products  31.4 us (8%)
  blocking collectives  31 us (8%)
  between operations  18 us (5%)
  starting transfers between devices  17.7 us (5%)
    another operation x14, other arithmetic, shards(): diag_factor = jnp.linalg.cholesky(top[lower:lower + PW, lower:lower + PW])  70.4 us
    all_gather x2, waiting for transfers between devices, shards(): gathered = lax.all_gather(panel, ('cube', 'front'), tiled=True)  46.6 us
    another operation x5, other arithmetic, shards(): lax.linalg.triangular_solve(diag_factor, eye, left_side=True, lower=True,...  42.8 us
    all_to_all x1, blocking collectives, shards(): scattered = lax.all_to_all(send, everyone, 0, 0, tiled=True)  31 us
    ppermute x3, waiting for transfers between devices, shards(): lax.ppermute(head_local, 'col', [(0, d)])  18 us
    all_to_all x1, waiting for transfers between devices, shards(): gathered_top = lax.all_to_all(spread_out, everyone, 0, 0, tiled=True)  17.4 us
    dot_general x2, matrix products, shards(): lax.dot_general(panel, col_panel, (((1,), (1,)), ((), ())), precision=HI)  13.9 us
    reshape x2, local copies, waits for them, and re-layouts, pick_columns(): shaped = block.reshape(n, halves, 2, grp)  13.8 us
  transfers between devices with their start and end apart: 7, of which 6 were waited for; matrix products, arithmetic and copies ran while one was open for 27% of the time, Pallas kernels for 0%

profile of v2, /device:TPU:1, one launch (start us, length us, event | category | flops | bytes accessed | tf_op | source)
XLA Modules:
  0.0 374.3 jit_solution(16615648167095741891)
XLA Ops:
  7.2 4.3 %constant_dynamic-slice_fusion.5 = (bf16[1,192,6144]{2,1,0:T(8,128)(2,1)S(1)}, bf16[1,192,6144]{2,1,0:T(8,128)(2,1)}) fusion(bf16[1,384,6144]{2,1,0:T(8,128)(2,1)} %param.8, s32[]{:T(128)S(6)} %select_n.158, s32[]{:T(128)S(6)} %select_n.161), kind=kLoop, calls=%fused_computation.114 | loop fusion | bytes 9437192 | tf_op jit(solution)/shard_map/dynamic_slice | solution.py:68
  11.4 9.0 %reshape.153 = bf16[192,16,2,192]{3,2,1,0:T(2,128)(2,1)} reshape(bf16[1,192,6144]{2,1,0:T(8,128)(2,1)} %get-tuple-element.53) | data formatting | bytes 4718592 | tf_op jit(solution)/shard_map/reshape | solution.py:25
  23.7 4.0 %collective-permute-start = (bf16[192,8,192]{2,1,0:T(8,128)(2,1)S(1)}, bf16[192,8,192]{2,1,0:T(8,128)(2,1)}, u32[]{:S(2)}, u32[]{:S(2)}) collective-permute-start(bf16[192,8,192]{2,1,0:T(8,128)(2,1)S(1)} %bitcast.111), channel_id=1, source_target_pairs={{0,64},{64,0},{1,65},{65,1},{2,66},{66,2},{3,67},{67,3},{4,68},{68... | collective-permute-start | bytes 1769480 | tf_op jit(solution)/shard_map/ppermute | solution.py:14
  27.7 4.8 %reshape.150 = bf16[192,16,2,192]{3,2,1,0:T(2,128)(2,1)} reshape(bf16[1,192,6144]{2,1,0:T(8,128)(2,1)S(1)} %get-tuple-element.52) | data formatting | bytes 4718592 | tf_op jit(solution)/shard_map/reshape | solution.py:25
  32.4 6.5 %dynamic-slice_reduce_fusion = bf16[192,8,192]{2,1,0:T(8,128)(2,1)S(1)} fusion(bf16[192,16,2,192]{3,2,1,0:T(2,128)(2,1)} %reshape.150, s32[]{:T(128)S(6)} %select_n.151, s32[]{:T(128)S(6)} %select_n.154), kind=kLoop, calls=%fused_computation.17 | loop fusion | bytes 1179656 | tf_op jit(solution)/shard_map/jit(dynamic_index_in_dim)/dynamic_slice | solution.py:29
  52.9 5.7 %collective-permute-start.1 = (f32[256,512]{0,1:T(8,128)}, f32[256,512]{0,1:T(8,128)S(1)}, u32[]{:S(2)}, u32[]{:S(2)}) collective-permute-start(f32[256,512]{0,1:T(8,128)} %slice.123), channel_id=1, source_target_pairs={{0,3},{4,7},{8,11},{12,15},{16,19},{20,23},{24,27},{28,31},{32,35}... | collective-permute-start | bytes 1572872 | tf_op jit(solution)/shard_map/ppermute | solution.py:91
  62.4 6.2 %collective-permute-done.1 = f32[256,512]{0,1:T(8,128)S(1)} collective-permute-done((f32[256,512]{0,1:T(8,128)}, f32[256,512]{0,1:T(8,128)S(1)}, u32[]{:S(2)}, u32[]{:S(2)}) %collective-permute-start.1) | collective-permute-done | bytes 524320 | tf_op jit(solution)/shard_map/ppermute | solution.py:91
  70.7 10.4 %collective-permute-done.3 = f32[256,512]{0,1:T(8,128)} collective-permute-done((f32[256,512]{0,1:T(8,128)}, f32[256,512]{0,1:T(8,128)}, u32[]{:S(2)}, u32[]{:S(2)}) %collective-permute-start.3) | collective-permute-done | bytes 524320 | tf_op jit(solution)/shard_map/ppermute | solution.py:91
  87.7 31.0 %all_to_all.21 = f32[128,1,2048]{2,1,0:T(1,128)S(1)} all-to-all(f32[128,1,2048]{2,1,0:T(1,128)S(1)} %copy.52), channel_id=1, replica_groups=mesh['cube'=2,'front'=16,'col'=4] {'cube','front','col'}, dimensions={0} | all-to-all | bytes 2097152 | tf_op jit(solution)/shard_map/all_to_all | solution.py:108
  120.5 4.1 %all-to-all-start.1 = ((f32[128,1,2048]{2,1,0:T(1,128)}), f32[128,1,2048]{2,1,0:T(1,128)S(1)}, u32[]{:S(2)}, u32[]{:S(2)}) async-start(f32[128,1,2048]{2,1,0:T(1,128)} %broadcast_in_dim.72), calls=%async_computation.1 | async-start | bytes 2097152 | tf_op jit(solution)/shard_map/all_to_all | solution.py:114
  126.5 17.4 %all-to-all-done.1 = f32[128,1,2048]{2,1,0:T(1,128)S(1)} async-done(((f32[128,1,2048]{2,1,0:T(1,128)}), f32[128,1,2048]{2,1,0:T(1,128)S(1)}, u32[]{:S(2)}, u32[]{:S(2)}) %all-to-all-start.1) | async-done | bytes 1048608 | tf_op jit(solution)/shard_map/all_to_all | solution.py:114
  153.7 11.7 %cholesky.130 = f32[128,128]{1,0:T(8,128)S(1)} custom-call(f32[128,128]{1,0:T(8,128)S(1)} %cholesky.194), custom_call_target="Cholesky" | custom-call | tf_op jit(solution)/shard_map/jit(cholesky)/cholesky | solution.py:126
  166.2 9.8 %custom-call.13 = f32[1,128,128]{1,2,0:T(8,128)S(1)} custom-call(f32[1,128,128]{2,1,0:T(8,128)S(1)} %get-tuple-element.70), custom_call_target="InvertDiagBlocksLowerTriangular" | custom-call | tf_op jit(solution)/shard_map/jit(cholesky)/cholesky | solution.py:126
  178.8 11.7 %cholesky.147 = f32[128,128]{1,0:T(8,128)S(1)} custom-call(f32[128,128]{1,0:T(8,128)S(1)} %convolution_subtract_fusion.4), custom_call_target="Cholesky" | custom-call | tf_op jit(solution)/shard_map/jit(cholesky)/cholesky | solution.py:126
  194.8 4.2 %while.4 = (s32[]{:T(128)}, f32[256,256]{1,0:T(8,128)S(1)}, s32[2,2]{1,0:T(2,128)S(1)}, f32[2,128,128]{2,1,0:T(8,128)S(1)}, s32[]{:T(128)}) while((s32[]{:T(128)}, f32[256,256]{1,0:T(8,128)S(1)}, s32[2,2]{1,0:T(2,128)S(1)}, f32[2,128,128]{2,1,0:T(8,128)S(1)}, s32[]{:T(128)}) %tuple.62), condition=%wide.while_cond, body=%wide.while_body.sunk | while | flops 2 | bytes 131189 | solution.py:127
  199.1 19.7 %custom-call.14 = f32[2,128,128]{1,2,0:T(8,128)S(1)} custom-call(f32[2,128,128]{2,1,0:T(8,128)S(1)} %get-tuple-element.18), custom_call_target="InvertDiagBlocksLowerTriangular" | custom-call | tf_op jit(solution)/shard_map/triangular_solve/custom-call.0 | solution.py:127
  229.1 11.7 %cholesky.164 = f32[128,128]{1,0:T(8,128)S(1)} custom-call(f32[128,128]{1,0:T(8,128)S(1)} %cholesky.197), custom_call_target="Cholesky" | custom-call | tf_op jit(solution)/shard_map/jit(cholesky)/cholesky | solution.py:126
  241.6 9.8 %custom-call.15 = f32[1,128,128]{1,2,0:T(8,128)S(1)} custom-call(f32[1,128,128]{2,1,0:T(8,128)S(1)} %get-tuple-element.66), custom_call_target="InvertDiagBlocksLowerTriangular" | custom-call | tf_op jit(solution)/shard_map/jit(cholesky)/cholesky | solution.py:126
  254.2 11.7 %cholesky.181 = f32[128,128]{1,0:T(8,128)S(1)} custom-call(f32[128,128]{1,0:T(8,128)S(1)} %convolution_subtract_fusion.3), custom_call_target="Cholesky" | custom-call | tf_op jit(solution)/shard_map/jit(cholesky)/cholesky | solution.py:126
  270.7 6.0 %while.5 = (s32[]{:T(128)}, f32[256,256]{1,0:T(8,128)}, s32[2,2]{1,0:T(2,128)S(1)}, f32[2,128,128]{2,1,0:T(8,128)S(1)}, s32[]{:T(128)}) while((s32[]{:T(128)}, f32[256,256]{1,0:T(8,128)}, s32[2,2]{1,0:T(2,128)S(1)}, f32[2,128,128]{2,1,0:T(8,128)S(1)}, s32[]{:T(128)}) %tuple.72), condition=%wide.while_cond.clone, body=%wide.while_body.clone.sunk | while | flops 2 | bytes 131189 | solution.py:127
  277.4 20.5 %custom-call.16 = f32[2,128,128]{1,2,0:T(8,128)S(1)} custom-call(f32[2,128,128]{2,1,0:T(8,128)} %copy-done.12), custom_call_target="InvertDiagBlocksLowerTriangular" | custom-call | tf_op jit(solution)/shard_map/triangular_solve/custom-call.0 | solution.py:127
  303.9 6.4 %fusion.5 = f32[256,2048]{0,1:T(8,128)} fusion(f32[256,256]{0,1:T(8,128)S(1)} %copy-done.1, f32[8192,256]{0,1:T(8,128)} %all-gather.3.cloned.1.call-done, s32[]{:T(128)S(6)} %select_n.181), kind=kOutput, calls=%fused_computation.14 | convolution fusion | flops 1610612736 | bytes 4456452 | tf_op jit(solution)/shard_map/dot_general | solution.py:140
  310.2 46.6 %all-gather.5.cloned.1.call-done = f32[8192,256]{0,1:T(8,128)} async-done(((f32[256,256]{0,1:T(8,128)}), f32[8192,256]{0,1:T(8,128)}) %all-gather.5.cloned.1.call-update) | async-done | bytes 8388624 | tf_op jit(solution)/shard_map/all_gather | solution.py:138
  356.9 7.5 %fusion.1 = f32[256,2048]{0,1:T(8,128)} fusion(f32[256,2048]{0,1:T(8,128)S(1)} %fusion.3, f32[256,2048]{0,1:T(8,128)} %fusion.5, f32[256,256]{0,1:T(8,128)S(1)} %copy-done.3, f32[8192,256]{0,1:T(8,128)} %all-gather.5.cloned.1.call-done, s32[]{:T(128)S(6)} %select_n.181, pred[256]{0:T(512)(128)(4,1)S(1)} %fusion.49, pred[2048]{0:T(1024)(128)(4,1)S(1)} %fusion.45), kind=kOutput, calls=%fused_computation.6 | convolution fusion | flops 1612709888 | bytes 8653060 | tf_op jit(solution)/shard_map/dot_general | solution.py:140
  (141 shorter events, 85.4 us)
Async XLA Ops:
  23.7 21.1 %collective-permute-start = (bf16[192,8,192]{2,1,0:T(8,128)(2,1)S(1)}, bf16[192,8,192]{2,1,0:T(8,128)(2,1)}, u32[]{:S(2)}, u32[]{:S(2)}) collective-permute-start(bf16[192,8,192]{2,1,0:T(8,128)(2,1)S(1)} %bitcast.111), channel_id=1, source_target_pairs={{0,64},{64,0},{1,65},{65,1},{2,66},{66,2},{3,67},{67,3},{4,68},{68... | collective-permute-start | bytes 1769480 | tf_op jit(solution)/shard_map/ppermute | solution.py:14
  32.4 7.8 %copy-start.13 = (s32[2,6144]{1,0:T(2,128)S(1)}, s32[2,6144]{1,0:T(2,128)}, u32[]{:S(2)}) copy-start(s32[2,6144]{1,0:T(2,128)} %param.9) | copy-start | bytes 147460
  48.5 1.6 copy-start
  52.9 15.7 %collective-permute-start.1 = (f32[256,512]{0,1:T(8,128)}, f32[256,512]{0,1:T(8,128)S(1)}, u32[]{:S(2)}, u32[]{:S(2)}) collective-permute-start(f32[256,512]{0,1:T(8,128)} %slice.123), channel_id=1, source_target_pairs={{0,3},{4,7},{8,11},{12,15},{16,19},{20,23},{24,27},{28,31},{32,35}... | collective-permute-start | bytes 1572872 | tf_op jit(solution)/shard_map/ppermute | solution.py:91
  58.6 11.3 %collective-permute-start.2 = (f32[256,512]{0,1:T(8,128)}, f32[256,512]{0,1:T(8,128)S(1)}, u32[]{:S(2)}, u32[]{:S(2)}) collective-permute-start(f32[256,512]{0,1:T(8,128)} %slice.123), channel_id=1, source_target_pairs={{0,2},{4,6},{8,10},{12,14},{16,18},{20,22},{24,26},{28,30},{32,34}... | collective-permute-start | bytes 1572872 | tf_op jit(solution)/shard_map/ppermute | solution.py:91
  59.9 21.3 %collective-permute-start.3 = (f32[256,512]{0,1:T(8,128)}, f32[256,512]{0,1:T(8,128)}, u32[]{:S(2)}, u32[]{:S(2)}) collective-permute-start(f32[256,512]{0,1:T(8,128)} %slice.123), channel_id=1, source_target_pairs={{0,1},{4,5},{8,9},{12,13},{16,17},{20,21},{24,25},{28,29},{32,33},... | collective-permute-start | bytes 1572872 | tf_op jit(solution)/shard_map/ppermute | solution.py:91
  68.6 1.3 copy-start.10
  69.9 0.8 copy-start.11
  120.5 23.4 %all-to-all-start.1 = ((f32[128,1,2048]{2,1,0:T(1,128)}), f32[128,1,2048]{2,1,0:T(1,128)S(1)}, u32[]{:S(2)}, u32[]{:S(2)}) async-start(f32[128,1,2048]{2,1,0:T(1,128)} %broadcast_in_dim.72), calls=%async_computation.1 | async-start | bytes 2097152 | tf_op jit(solution)/shard_map/all_to_all | solution.py:114
  124.7 179.2 %all-gather.3.cloned.1.call-start = ((), (), s32[]{:S(2)}) async-start(), calls=%async_computation.2 | async-start | bytes 8650752 | tf_op jit(solution)/shard_map/all_gather | solution.py:138
  124.7 94.3 %copy-start.5 = (f32[256,256]{1,0:T(8,128)}, f32[256,256]{1,0:T(8,128)S(1)}, u32[]{:S(2)}) copy-start(f32[256,256]{1,0:T(8,128)S(1)} %fusion.28) | copy-start | bytes 786436
  148.6 29.1 %copy-start.2 = (f32[256,512]{0,1:T(8,128)}, f32[256,512]{0,1:T(8,128)S(1)}, u32[]{:S(2)}) copy-start(f32[256,512]{0,1:T(8,128)S(1)} %copy.54) | copy-start | bytes 1572868
  153.0 0.7 copy-start.9
  222.4 134.5 %all-gather.5.cloned.1.call-start = ((), (), s32[]{:S(2)}) async-start(), calls=%async_computation.3 | async-start | bytes 8650752 | tf_op jit(solution)/shard_map/all_gather | solution.py:138
  224.6 1.0 copy-start.4
  226.3 71.6 %copy-start.6 = (f32[256,256]{1,0:T(8,128)S(1)}, f32[256,256]{1,0:T(8,128)}, u32[]{:S(2)}) copy-start(f32[256,256]{1,0:T(8,128)} %copy-done.5) | copy-start | bytes 786436
  228.4 0.7 copy-start.8
  229.1 70.5 %copy-start.1 = (f32[256,256]{0,1:T(8,128)S(1)}, f32[256,256]{0,1:T(8,128)}, u32[]{:S(2)}) copy-start(f32[256,256]{0,1:T(8,128)} %slice_select_fusion) | copy-start | bytes 786436
  276.7 0.7 copy-start.12
  297.9 2.8 copy-start.7
  297.9 2.8 slice-start
  303.8 53.0 %copy-start.3 = (f32[256,256]{0,1:T(8,128)S(1)}, f32[256,256]{0,1:T(8,128)}, u32[]{:S(2)}) copy-start(f32[256,256]{0,1:T(8,128)} %convolution_select_fusion) | copy-start | bytes 786436
Sparse Core Ops, SparseCore 0:
  222.5 55.1 all-gather.2
  302.0 54.8 all-gather.4
